TPU v7x, 32 devices: a whole 2x2x4 slice. The times are simulated.
32 devices in a mesh: groups: 2 (over y), ctx: 4 (over z), head: 2 (over x), rep: 2 (over core).
Axes of the slice: x: 2, y: 2, z: 4, core: 2. Of those that a mesh axis runs over, the one named last changes fastest.
Arguments:
- query: bfloat16 [2048, 4096], P(('groups', 'ctx', 'rep'), 'head'), parts along dimension 0, may hold values from -23.069359 to 23.069359
- key: bfloat16 [4096, 1024], P(('groups', 'ctx'), 'head'), parts along dimension 0, may hold values from -6 to 6
- value: bfloat16 [4096, 1024], P(('groups', 'ctx'), 'head'), parts along dimension 0, may hold values from -24 to 24
- out_weight: bfloat16 [4096, 4096], P('head'), may hold values from -0.375 to 0.375
- cotangent: bfloat16 [2048, 4096], P(('groups', 'ctx', 'rep')), parts along dimension 0, may hold values from -6 to 6
- response: int32 [2048], P(('groups', 'ctx', 'rep')), parts along dimension 0, may hold values 0 or 1
- segment_ids: int32 [4096], P(('groups', 'ctx')), parts along dimension 0, may hold values from 0 to 31, never falling along the last dimension, each value on 1 to 128 neighbouring positions
- masked_segments: int32 [8], P('groups'), parts along dimension 0, may hold values from 0 to 31
Outputs:
- patch_effect: bfloat16 [2048, 4096], P(('groups', 'ctx', 'rep'), 'head'), parts along dimension 0
- token_attr: float32 [4096], P(('groups', 'ctx')), parts along dimension 0
- segment_attr: float32 [64], P('groups'), parts along dimension 0
There are 2 independent parts, one for each index of `groups`. A program takes and returns all parts, laid end to end along the dimension named above; an argument that names none is the same for every part. Nothing has to cross between parts.
All inputs are finite; a program needn't handle non-finite values. No bound on the sum of `response` on one device may be relied on, other than what follows from the above.
Results may differ from a plain program's by a relative error of at most 0.0095.
Values may be sent and summed in bfloat16 or wider, within the bound.
No kernel may reach another device: no remote copies, remote signals or barrier semaphores. Data moves between devices by JAX's collectives and lax.ppermute only.
A program may use at most 128 MiB of HBM per device.

v0:
```python
from functools import partial
import jax
import jax.numpy as jnp
from jax import lax
from jax.sharding import PartitionSpec as P

HD = 128
SEG_DEV = 8
NEG_FILL = -1e30


def split_heads(incoming):
    return incoming.reshape(incoming.shape[0], -1, HD)


def block_scores(query_rows, key_block):
    raw_scores = jnp.einsum(
        "gqd,tgd->gqt", query_rows, split_heads(key_block), preferred_element_type=jnp.float32
    )
    return raw_scores * HD ** (-0.5)


def visible_keys(row_pos, first_key, key_rows):
    key_pos = first_key + jnp.arange(key_rows, dtype=jnp.int32)
    return key_pos[None, None, :] <= row_pos[None, :, None]


def online_update(running, scores, allowed, value_heads):
    row_top, row_total, weighted = running
    chosen = jnp.where(allowed, scores, NEG_FILL)
    new_top = jnp.maximum(row_top, jnp.max(chosen, axis=2))
    shrink = jnp.exp(row_top - new_top)
    weights = jnp.where(allowed, jnp.exp(chosen - new_top[:, :, None]), 0.0)
    row_total = row_total * shrink + jnp.sum(weights, axis=2)
    weighted = weighted * shrink[:, :, None] + jnp.einsum(
        "gqt,tgd->gqd",
        weights.astype(jnp.bfloat16),
        value_heads,
        preferred_element_type=jnp.float32,
    )
    return (new_top, row_total, weighted)


def forward_piece(query_rows, row_pos, running, incoming, first_key):
    key_block, value_block, kept_flag = incoming
    scores = block_scores(query_rows, key_block)
    visible = visible_keys(row_pos, first_key, key_block.shape[0])
    kept_visible = jnp.logical_and(visible, kept_flag[None, None, :] > 0)
    value_heads = split_heads(value_block)
    return (
        online_update(running[0], scores, visible, value_heads),
        online_update(running[1], scores, kept_visible, value_heads),
    )


def backward_terms(
    query_rows, row_pos, grad_rows, log_total, row_dot, key_block, value_block, first_key
):
    scores = block_scores(query_rows, key_block)
    visible = visible_keys(row_pos, first_key, key_block.shape[0])
    shifted = jnp.where(visible, scores - log_total[:, :, None], 0.0)
    probability = jnp.where(visible, jnp.exp(shifted), 0.0)
    grad_prob = jnp.einsum(
        "gqd,tgd->gqt", grad_rows, split_heads(value_block), preferred_element_type=jnp.float32
    )
    return jnp.sum(
        probability * (grad_prob + (grad_prob - row_dot[:, :, None]) * shifted), axis=(0, 1)
    )


def blockwise(stepper, state_in, incoming, block_rows):
    length = jax.tree.leaves(incoming)[0].shape[0]

    def advance(counter, state_now):
        offset = counter * block_rows
        portion = jax.tree.map(
            lambda member: lax.dynamic_slice_in_dim(member, offset, block_rows, 0), incoming
        )
        return stepper(state_now, portion, offset)

    return lax.fori_loop(0, length // block_rows, advance, state_in)


def finish_pass(running):
    row_top, row_total, weighted = running
    return (weighted / row_total[:, :, None], row_top + jnp.log(row_total))


def local(query, key, value, out_weight, cotangent, response, segment_ids, masked_segments):
    ctx_count = lax.axis_size("ctx")
    rep_count = lax.axis_size("rep")
    ctx_at = lax.axis_index("ctx")
    rep_at = lax.axis_index("rep")
    query_count = query.shape[0]
    key_count = key.shape[0]
    kv_local = key.shape[1] // HD
    heads_local = query.shape[1] // HD
    group_size = heads_local // kv_local
    context_len = key_count * ctx_count
    query_base = context_len - query_count * ctx_count * rep_count
    row_width = group_size * query_count
    kept_flag = jnp.where(
        jnp.any(segment_ids[:, None] == masked_segments[None, :], axis=1), 0.0, 1.0
    ).astype(jnp.bfloat16)
    grad_masked = jnp.where(response[:, None] > 0, cotangent, jnp.zeros_like(cotangent))
    grad_out = jnp.dot(grad_masked, out_weight.T, preferred_element_type=jnp.float32).astype(
        jnp.bfloat16
    )

    def grouped(rows_in):
        return rows_in.reshape(query_count, kv_local, group_size, HD).transpose(1, 2, 0, 3)

    fresh_state = (
        jnp.full((kv_local, row_width), NEG_FILL, jnp.float32),
        jnp.zeros((kv_local, row_width), jnp.float32),
        jnp.zeros((kv_local, row_width, HD), jnp.float32),
    )
    starting = (fresh_state, fresh_state)
    query_rows = grouped(query).reshape(kv_local, row_width, HD)
    grad_own = grouped(grad_out).reshape(kv_local, row_width, HD)
    base_pos = (
        query_base
        + (ctx_at * rep_count + rep_at) * query_count
        + jnp.arange(query_count, dtype=jnp.int32)
    )
    own_pos = jnp.tile(base_pos, group_size)
    forward_step = partial(forward_piece, query_rows, own_pos)
    running = blockwise(
        forward_step,
        starting,
        (
            lax.all_gather(key, "ctx", axis=0, tiled=True),
            lax.all_gather(value, "ctx", axis=0, tiled=True),
            lax.all_gather(kept_flag, "ctx", axis=0, tiled=True),
        ),
        key_count,
    )
    clean_out, log_total = finish_pass(running[0])
    masked_out, _ = finish_pass(running[1])
    row_dot = jnp.sum(grad_own.astype(jnp.float32) * clean_out, axis=2)

    def backward_step(total_now, incoming, first_key):
        added = backward_terms(
            query_rows, own_pos, grad_own, log_total, row_dot, incoming[0], incoming[1], first_key
        )
        current = lax.dynamic_slice_in_dim(total_now, first_key, incoming[0].shape[0], 0)
        return lax.dynamic_update_slice_in_dim(total_now, current + added, first_key, 0)

    empty_attr = jnp.zeros((context_len,), jnp.float32)
    attr_all = blockwise(
        backward_step,
        empty_attr,
        (
            lax.all_gather(key, "ctx", axis=0, tiled=True),
            lax.all_gather(value, "ctx", axis=0, tiled=True),
        ),
        key_count,
    )
    local_attr = lax.psum_scatter(attr_all, "ctx", scatter_dimension=0, tiled=True)
    change = (
        (masked_out - clean_out)
        .reshape(kv_local, group_size, query_count, HD)
        .transpose(2, 0, 1, 3)
        .reshape(query_count, heads_local * HD)
        .astype(jnp.bfloat16)
    )
    projected = jnp.dot(change, out_weight, preferred_element_type=jnp.float32)
    patch_effect = lax.psum_scatter(projected, "head", scatter_dimension=1, tiled=True).astype(
        jnp.bfloat16
    )
    token_attr = lax.psum(local_attr, ("head", "rep"))
    onehot = (
        segment_ids[:, None] == jnp.arange(SEG_DEV * ctx_count, dtype=jnp.int32)[None, :]
    ).astype(jnp.float32)
    segment_attr = lax.psum(jnp.dot(token_attr, onehot, precision=lax.Precision.HIGHEST), "ctx")
    return (patch_effect, token_attr, segment_attr)


def solution(mesh):
    return jax.shard_map(
        local,
        mesh=mesh,
        in_specs=(
            P(("groups", "ctx", "rep"), "head"),
            P(("groups", "ctx"), "head"),
            P(("groups", "ctx"), "head"),
            P("head", None),
            P(("groups", "ctx", "rep"), None),
            P(("groups", "ctx", "rep")),
            P(("groups", "ctx")),
            P("groups"),
        ),
        out_specs=(P(("groups", "ctx", "rep"), "head"), P(("groups", "ctx")), P("groups")),
        check_vma=False,
    )
```

profile of v0, /device:TPU:0, one launch (start us, length us, event | category | flops | bytes accessed | tf_op | source)
XLA Modules:
  0.0 224.0 jit_solution(5980120812336782876)
XLA Ops:
  7.3 2.1 copy.57
  9.5 2.0 copy.59
  11.6 1.4 reshape.201
  13.3 13.7 %all-gather = bf16[4,1,512]{2,1,0:T(2,128)(2,1)S(1)} all-gather(bf16[1,1,512]{2,1,0:T(2,128)(2,1)S(1)} %reshape.205), channel_id=1, replica_groups=mesh['groups'=2,'ctx'=4,'head'=2,'rep'=2] {'ctx'}, dimensions={0}, use_global_device_ids=true | all-gather | bytes 5120 | tf_op jit(solution)/shard_map/all_gather | solution.py:134
  27.1 11.5 %convolution_convert_fusion = bf16[128,2048]{1,0:T(8,128)(2,1)S(1)} fusion(bf16[2048,4096]{1,0:T(8,128)(2,1)} %param.15, bf16[128,4096]{1,0:T(8,128)(2,1)S(1)} %copy-done.3, pred[128]{0:T(512)(128)(4,1)S(1)} %broadcast_compare_fusion.2), kind=kOutput, calls=%fused_computation.53 | convolution fusion | flops 2148270080 | bytes 18350208 | tf_op jit(solution)/shard_map/dot_general | solution.py:106
  38.6 0.4 reshape.203
  39.2 0.7 dynamic-slice
  40.5 18.3 %all-gather.4.cloned.1.call-done = bf16[2048,512]{0,1:T(8,128)(2,1)} async-done(((bf16[512,512]{0,1:T(8,128)(2,1)}), bf16[2048,512]{0,1:T(8,128)(2,1)}) %all-gather.4.cloned.1.call-update) | async-done | bytes 2097168 | tf_op jit(solution)/shard_map/all_gather | solution.py:132
  58.9 46.4 %all-gather.6.cloned.1.call-done = bf16[2048,512]{0,1:T(8,128)(2,1)} async-done(((bf16[512,512]{0,1:T(8,128)(2,1)}), bf16[2048,512]{0,1:T(8,128)(2,1)}) %all-gather.6.cloned.1.call-update) | async-done | bytes 2097168 | tf_op jit(solution)/shard_map/all_gather | solution.py:133
  105.2 54.5 %while.39 = (s32[]{:T(128)}, f32[4,512]{1,0:T(4,128)S(1)}, f32[4,512]{1,0:T(4,128)S(1)}, f32[4,512,128]{2,1,0:T(8,128)S(1)}, f32[4,512]{1,0:T(4,128)S(1)}, /*ind...) while((s32[]{:T(128)}, f32[4,512]{1,0:T(4,128)S(1)}, ...), condition=%wide.region_6.7_spmd.clone, body=%wide.region_1.6_spmd.clone.sunk | while | flops 832591872 | bytes 52702004 | solution.py:81
  105.3 0.3 broadcast_compare_fusion.6
  105.6 1.1 constant_dynamic-slice_fusion.8
  106.7 3.4 %fusion.81 = (f32[4,512]{1,0:T(4,128)S(1)}, f32[4,512]{1,0:T(4,128)S(1)}, f32[4,512,512]{2,1,0:T(8,128)}) fusion(pred[512,512]{0,1:T(8,128)(4,1)S(1)} %get-tuple-element.631, pred[512,512]{0,1:T(8,128)(4,1)S(1)} %get-tuple-element.632, bf16[512,4,128]{0,2,1:T(8,128)(2,1)S(1)} %bitcast.121, bf16[4,512,128]{2,1,0:T(8,128)(2,1)S(1)} %get-tuple-element.682), kind=kOutput, calls=%fused_computation.19.clone.1 | convolution fusion | flops 273674240 | bytes 5783552 | tf_op jit(solution)/shard_map/while/body/eval_jaxpr/gqd,tgd->gqt/dot_general | solution.py:17
  110.1 3.7 %fusion.82 = (f32[4,512]{1,0:T(4,128)S(1)}, f32[4,512]{1,0:T(4,128)S(1)}) fusion(f32[4,512,512]{2,1,0:T(8,128)} %get-tuple-element.634, f32[4,512]{1,0:T(4,128)S(1)} %select_maximum_fusion.5, pred[512,512]{0,1:T(8,128)(4,1)S(1)} %get-tuple-element.631, f32[4,512]{1,0:T(4,128)S(1)} %select_maximum_fusion.4, pred[512,512]{0,1:T(8,128)(4,1)S(1)} %get-tuple-element.632), kind=kLoop, calls=%fused_computation.23.clone.1 | loop fusion | flops 9433088 | bytes 4751360 | tf_op jit(solution)/shard_map/while/body/eval_jaxpr/reduce_sum | solution.py:34
  113.9 1.1 constant_dynamic-slice_fusion.9
  115.0 1.9 fusion.85
  116.9 1.9 fusion.84
  119.0 0.3 broadcast_compare_fusion.6
  119.3 1.1 constant_dynamic-slice_fusion.8
  120.4 3.4 %fusion.81 = (f32[4,512]{1,0:T(4,128)S(1)}, f32[4,512]{1,0:T(4,128)S(1)}, f32[4,512,512]{2,1,0:T(8,128)}) fusion(pred[512,512]{0,1:T(8,128)(4,1)S(1)} %get-tuple-element.631, pred[512,512]{0,1:T(8,128)(4,1)S(1)} %get-tuple-element.632, bf16[512,4,128]{0,2,1:T(8,128)(2,1)S(1)} %bitcast.121, bf16[4,512,128]{2,1,0:T(8,128)(2,1)S(1)} %get-tuple-element.682), kind=kOutput, calls=%fused_computation.19.clone.1 | convolution fusion | flops 273674240 | bytes 5783552 | tf_op jit(solution)/shard_map/while/body/eval_jaxpr/gqd,tgd->gqt/dot_general | solution.py:17
  123.8 3.7 %fusion.82 = (f32[4,512]{1,0:T(4,128)S(1)}, f32[4,512]{1,0:T(4,128)S(1)}) fusion(f32[4,512,512]{2,1,0:T(8,128)} %get-tuple-element.634, f32[4,512]{1,0:T(4,128)S(1)} %select_maximum_fusion.5, pred[512,512]{0,1:T(8,128)(4,1)S(1)} %get-tuple-element.631, f32[4,512]{1,0:T(4,128)S(1)} %select_maximum_fusion.4, pred[512,512]{0,1:T(8,128)(4,1)S(1)} %get-tuple-element.632), kind=kLoop, calls=%fused_computation.23.clone.1 | loop fusion | flops 9433088 | bytes 4751360 | tf_op jit(solution)/shard_map/while/body/eval_jaxpr/reduce_sum | solution.py:34
  127.5 1.1 constant_dynamic-slice_fusion.9
  128.6 1.9 fusion.85
  130.6 1.9 fusion.84
  132.6 0.3 broadcast_compare_fusion.6
  132.9 1.1 constant_dynamic-slice_fusion.8
  134.0 3.4 %fusion.81 = (f32[4,512]{1,0:T(4,128)S(1)}, f32[4,512]{1,0:T(4,128)S(1)}, f32[4,512,512]{2,1,0:T(8,128)}) fusion(pred[512,512]{0,1:T(8,128)(4,1)S(1)} %get-tuple-element.631, pred[512,512]{0,1:T(8,128)(4,1)S(1)} %get-tuple-element.632, bf16[512,4,128]{0,2,1:T(8,128)(2,1)S(1)} %bitcast.121, bf16[4,512,128]{2,1,0:T(8,128)(2,1)S(1)} %get-tuple-element.682), kind=kOutput, calls=%fused_computation.19.clone.1 | convolution fusion | flops 273674240 | bytes 5783552 | tf_op jit(solution)/shard_map/while/body/eval_jaxpr/gqd,tgd->gqt/dot_general | solution.py:17
  137.4 3.7 %fusion.82 = (f32[4,512]{1,0:T(4,128)S(1)}, f32[4,512]{1,0:T(4,128)S(1)}) fusion(f32[4,512,512]{2,1,0:T(8,128)} %get-tuple-element.634, f32[4,512]{1,0:T(4,128)S(1)} %select_maximum_fusion.5, pred[512,512]{0,1:T(8,128)(4,1)S(1)} %get-tuple-element.631, f32[4,512]{1,0:T(4,128)S(1)} %select_maximum_fusion.4, pred[512,512]{0,1:T(8,128)(4,1)S(1)} %get-tuple-element.632), kind=kLoop, calls=%fused_computation.23.clone.1 | loop fusion | flops 9433088 | bytes 4751360 | tf_op jit(solution)/shard_map/while/body/eval_jaxpr/reduce_sum | solution.py:34
  141.2 1.1 constant_dynamic-slice_fusion.9
  142.3 1.9 fusion.85
  144.2 1.9 fusion.84
  146.2 0.3 broadcast_compare_fusion.6
  146.6 1.1 constant_dynamic-slice_fusion.8
  147.7 3.4 %fusion.81 = (f32[4,512]{1,0:T(4,128)S(1)}, f32[4,512]{1,0:T(4,128)S(1)}, f32[4,512,512]{2,1,0:T(8,128)}) fusion(pred[512,512]{0,1:T(8,128)(4,1)S(1)} %get-tuple-element.631, pred[512,512]{0,1:T(8,128)(4,1)S(1)} %get-tuple-element.632, bf16[512,4,128]{0,2,1:T(8,128)(2,1)S(1)} %bitcast.121, bf16[4,512,128]{2,1,0:T(8,128)(2,1)S(1)} %get-tuple-element.682), kind=kOutput, calls=%fused_computation.19.clone.1 | convolution fusion | flops 273674240 | bytes 5783552 | tf_op jit(solution)/shard_map/while/body/eval_jaxpr/gqd,tgd->gqt/dot_general | solution.py:17
  151.1 3.7 %fusion.82 = (f32[4,512]{1,0:T(4,128)S(1)}, f32[4,512]{1,0:T(4,128)S(1)}) fusion(f32[4,512,512]{2,1,0:T(8,128)} %get-tuple-element.634, f32[4,512]{1,0:T(4,128)S(1)} %select_maximum_fusion.5, pred[512,512]{0,1:T(8,128)(4,1)S(1)} %get-tuple-element.631, f32[4,512]{1,0:T(4,128)S(1)} %select_maximum_fusion.4, pred[512,512]{0,1:T(8,128)(4,1)S(1)} %get-tuple-element.632), kind=kLoop, calls=%fused_computation.23.clone.1 | loop fusion | flops 9433088 | bytes 4751360 | tf_op jit(solution)/shard_map/while/body/eval_jaxpr/reduce_sum | solution.py:34
  154.8 1.1 constant_dynamic-slice_fusion.9
  155.9 1.9 fusion.85
  157.8 1.9 fusion.84
  159.8 2.1 multiply_reduce_fusion
  162.0 0.3 copy.60
  162.2 9.5 %fusion.39 = f32[128,4096]{1,0:T(8,128)} fusion(bf16[128,2048]{0,1:T(8,128)(2,1)S(1)} %bitcast.122, bf16[2048,4096]{1,0:T(8,128)(2,1)} %param.15), kind=kOutput, calls=%fused_computation.70 | convolution fusion | flops 2147483648 | bytes 19398656 | tf_op jit(solution)/shard_map/dot_general | solution.py:167
  171.8 18.3 %while.38 = (s32[]{:T(128)}, f32[2048]{0:T(1024)S(1)}, bf16[2048,512]{0,1:T(8,128)(2,1)}, bf16[4,512,128]{2,1,0:T(8,128)(2,1)S(1)}, f32[4,512]{1,0:T(4,128)S(1)}...) while((s32[]{:T(128)}, f32[2048]{0:T(1024)S(1)}, ...), condition=%wide.region_11.12_spmd.clone, body=%wide.region_9.11_spmd.clone.sunk | while | flops 546570752 | bytes 13140663 | solution.py:81
  171.8 1.3 constant_dynamic-slice_fusion.7
  173.1 0.7 fusion.73
  173.8 0.2 broadcast_compare_fusion.5
  174.0 2.1 fusion.74
  176.1 0.2 add_dynamic-update-slice_fusion.2
  176.3 1.5 constant_dynamic-slice_fusion.7
  177.8 0.7 fusion.73
  178.5 0.2 broadcast_compare_fusion.5
  178.7 2.1 fusion.74
  181.0 1.3 constant_dynamic-slice_fusion.7
  182.3 0.7 fusion.73
  183.0 0.2 broadcast_compare_fusion.5
  183.2 2.1 fusion.74
  185.5 1.3 constant_dynamic-slice_fusion.7
  186.8 0.7 fusion.73
  187.5 0.2 broadcast_compare_fusion.5
  187.7 2.1 fusion.74
  190.0 9.4 %all-reduce = f32[2048]{0:T(1024)S(1)} all-reduce(f32[2048]{0:T(1024)S(1)} %get-tuple-element.365), channel_id=3, replica_groups=mesh['groups'=2,'ctx'=4,'head'=2,'rep'=2] {'ctx'}, use_global_device_ids=true, to_apply=%region_12.13.clone | all-reduce | flops 2048 | bytes 16384
  199.5 5.6 %psum.14 = f32[512]{0:T(512)S(1)} all-reduce(f32[512]{0:T(512)S(1)} %dynamic-slice.1), channel_id=1, replica_groups=mesh['groups'=2,'ctx'=4,'head'=2,'rep'=2] {'head','rep'}, use_global_device_ids=true, to_apply=%region_13.14 | all-reduce | flops 512 | bytes 4096 | tf_op jit(solution)/shard_map/psum | solution.py:171
  205.1 0.3 convolution_bitcast_fusion
  205.4 10.0 %psum.15 = f32[32]{0:T(128)} all-reduce(f32[32]{0:T(128)S(1)} %convolution_bitcast_fusion), channel_id=1, replica_groups=mesh['groups'=2,'ctx'=4,'head'=2,'rep'=2] {'ctx'}, use_global_device_ids=true, to_apply=%region_14.15 | all-reduce | flops 32 | bytes 256 | tf_op jit(solution)/shard_map/psum | solution.py:175
  215.4 2.1 convert_element_type.44
  (104 shorter events, 1.9 us)
Async XLA Ops:
  7.2 6.0 %copy-start.4 = (s32[512]{0:T(512)S(1)}, s32[512]{0:T(512)}, u32[]{:S(2)}) copy-start(s32[512]{0:T(512)} %param.18) | copy-start | bytes 6148
  7.2 6.0 %copy-start.6 = (s32[4]{0:T(128)S(1)}, s32[4]{0:T(128)}, u32[]{:S(2)}) copy-start(s32[4]{0:T(128)} %param.19) | copy-start | bytes 52
  7.2 19.9 %copy-start.7 = (s32[128]{0:T(128)S(1)}, s32[128]{0:T(128)}, u32[]{:S(2)}) copy-start(s32[128]{0:T(128)} %param.17) | copy-start | bytes 1540
  7.2 19.9 %copy-start.3 = (bf16[128,4096]{1,0:T(8,128)(2,1)S(1)}, bf16[128,4096]{1,0:T(8,128)(2,1)}, u32[]{:S(2)}) copy-start(bf16[128,4096]{1,0:T(8,128)(2,1)} %param.16) | copy-start | bytes 3145732
  7.2 51.7 %all-gather.4.cloned.1.call-start = ((), (), s32[]{:S(2)}) async-start(), calls=%async_computation.1 | async-start | bytes 2621440 | tf_op jit(solution)/shard_map/all_gather | solution.py:132
  9.4 95.8 %all-gather.6.cloned.1.call-start = ((), (), s32[]{:S(2)}) async-start(), calls=%async_computation.2 | async-start | bytes 2621440 | tf_op jit(solution)/shard_map/all_gather | solution.py:133
  11.5 203.9 %reduce-scatter.2.cloned.1.call-start = ((), (), s32[]{:S(2)}) async-start(), calls=%async_computation.3 | async-start | bytes 3145728 | tf_op jit(solution)/shard_map/reduce_scatter | solution.py:168
  27.1 12.1 %copy-start.8 = (u32[32]{0:T(128)S(1)}, u32[32]{0:T(128)}, u32[]{:S(2)}) copy-start(u32[32]{0:T(128)} %constant.131) | copy-start | bytes 388
  110.1 4.9 %copy-start = (f32[4,512,512]{2,1,0:T(8,128)S(1)}, f32[4,512,512]{2,1,0:T(8,128)}, u32[]{:S(2)}) copy-start(f32[4,512,512]{2,1,0:T(8,128)} %get-tuple-element.634) | copy-start | bytes 12582916 | tf_op jit(solution)/shard_map/while
  110.1 4.9 %copy-start.1 = (f32[4,512,128]{2,1,0:T(8,128)S(1)}, f32[4,512,128]{2,1,0:T(8,128)}, u32[]{:S(2)}) copy-start(f32[4,512,128]{2,1,0:T(8,128)} %get-tuple-element.664) | copy-start | bytes 3145732 | tf_op jit(solution)/shard_map/while
  116.9 1.9 copy-start.2
  123.8 4.9 %copy-start = (f32[4,512,512]{2,1,0:T(8,128)S(1)}, f32[4,512,512]{2,1,0:T(8,128)}, u32[]{:S(2)}) copy-start(f32[4,512,512]{2,1,0:T(8,128)} %get-tuple-element.634) | copy-start | bytes 12582916 | tf_op jit(solution)/shard_map/while
  123.8 4.9 %copy-start.1 = (f32[4,512,128]{2,1,0:T(8,128)S(1)}, f32[4,512,128]{2,1,0:T(8,128)}, u32[]{:S(2)}) copy-start(f32[4,512,128]{2,1,0:T(8,128)} %get-tuple-element.664) | copy-start | bytes 3145732 | tf_op jit(solution)/shard_map/while
  130.6 1.9 copy-start.2
  137.4 4.9 %copy-start = (f32[4,512,512]{2,1,0:T(8,128)S(1)}, f32[4,512,512]{2,1,0:T(8,128)}, u32[]{:S(2)}) copy-start(f32[4,512,512]{2,1,0:T(8,128)} %get-tuple-element.634) | copy-start | bytes 12582916 | tf_op jit(solution)/shard_map/while
  137.4 4.9 %copy-start.1 = (f32[4,512,128]{2,1,0:T(8,128)S(1)}, f32[4,512,128]{2,1,0:T(8,128)}, u32[]{:S(2)}) copy-start(f32[4,512,128]{2,1,0:T(8,128)} %get-tuple-element.664) | copy-start | bytes 3145732 | tf_op jit(solution)/shard_map/while
  144.2 1.9 copy-start.2
  151.0 4.9 %copy-start = (f32[4,512,512]{2,1,0:T(8,128)S(1)}, f32[4,512,512]{2,1,0:T(8,128)}, u32[]{:S(2)}) copy-start(f32[4,512,512]{2,1,0:T(8,128)} %get-tuple-element.634) | copy-start | bytes 12582916 | tf_op jit(solution)/shard_map/while
  151.0 4.9 %copy-start.1 = (f32[4,512,128]{2,1,0:T(8,128)S(1)}, f32[4,512,128]{2,1,0:T(8,128)}, u32[]{:S(2)}) copy-start(f32[4,512,128]{2,1,0:T(8,128)} %get-tuple-element.664) | copy-start | bytes 3145732 | tf_op jit(solution)/shard_map/while
  157.8 1.9 copy-start.2
  205.1 12.4 %copy-start.5 = (f32[512]{0:T(512)}, f32[512]{0:T(512)S(1)}, u32[]{:S(2)}) copy-start(f32[512]{0:T(512)S(1)} %psum.14) | copy-start | bytes 6148
Sparse Core Ops, SparseCore 0:
  10.2 48.6 all-gather.3
  60.4 44.7 all-gather.5
  171.9 30.5 reduce-scatter.1
where the time goes:
time: 225 us; the launch traced here: 224 us
  waiting for transfers between devices  64.7 us (29%)
  matrix products  61.2 us (27%)
  blocking collectives  38.7 us (17%)
  other arithmetic  22.6 us (10%)
  local copies, waits for them, and re-layouts  21.4 us (10%)
  between operations  14.7 us (7%)
    all_gather x1, waiting for transfers between devices, local(): lax.all_gather(value, 'ctx', axis=0, tiled=True)  46.4 us
    all_gather x1, waiting for transfers between devices, local(): lax.all_gather(key, 'ctx', axis=0, tiled=True)  18.3 us
    dot_general x8, matrix products, block_scores(): jnp.einsum('gqd,tgd->gqt', query_rows, split_heads(key_block), preferred_...  16.3 us
    dot_general x8, matrix products, online_update(): jnp.einsum('gqt,tgd->gqd', weights.astype(jnp.bfloat16), value_heads, pre...  15.3 us
    reduce_sum x4, other arithmetic, online_update(): row_total = row_total * shrink + jnp.sum(weights, axis=2)  14.8 us
    dynamic_slice x12, local copies, waits for them, and re-layouts, advance(): lax.dynamic_slice_in_dim(member, offset, block_rows, 0)  14 us
    all_gather x1, blocking collectives, local(): lax.all_gather(kept_flag, 'ctx', axis=0, tiled=True)  13.7 us
    dot_general x1, matrix products, local(): jnp.dot(grad_masked, out_weight.T, preferred_element_type=jnp.float32)  11.5 us
  transfers between devices with their start and end apart: 3, of which 2 were waited for; matrix products, arithmetic and copies ran while one was open for 16% of the time, Pallas kernels for 0%

commit v1 on v0

--- a/solution.py
+++ b/solution.py
@@ -7,6 +7,17 @@
 HD = 128
 SEG_DEV = 8
 NEG_FILL = -1e30
+
+
+def ring_gather(shard, axis, dim):
+    ways = lax.axis_size(axis)
+    pieces = [shard]
+    for far in range(1, ways):
+        pieces.append(
+            lax.ppermute(pieces[far - 1], axis, [(d, (d - 1) % ways) for d in range(ways)])
+        )
+    line = jnp.concatenate(pieces, axis=dim)
+    return jnp.roll(line, lax.axis_index(axis) * shard.shape[dim], axis=dim)
 
 
 def split_heads(incoming):
@@ -129,7 +140,7 @@
         forward_step,
         starting,
         (
-            lax.all_gather(key, "ctx", axis=0, tiled=True),
+            ring_gather(key, "ctx", 0),
             lax.all_gather(value, "ctx", axis=0, tiled=True),
             lax.all_gather(kept_flag, "ctx", axis=0, tiled=True),
         ),

time: 225 us -> 216 us (0.960)
  waiting for transfers between devices: 64.7 us -> 37.7 us
  starting transfers between devices: 0.12 us -> 9.56 us
  blocking collectives: 38.7 us -> 45.1 us
    all_gather x1, waiting for transfers between devices: 46.4 us -> 0.02 us  [local(): lax.all_gather(value, 'ctx', axis=0, tiled=True)]
    ppermute x0 -> x3, waiting for transfers between devices: none -> 37.6 us  [ring_gather(): lax.ppermute(pieces[far - 1], axis, [(d, (d - 1) % ways) for d in range(w...]
    all_gather x1, waiting for transfers between devices: 18.3 us -> 0.02 us  [local(): lax.all_gather(key, 'ctx', axis=0, tiled=True)]
    ppermute x0 -> x3, starting transfers between devices: none -> 9.44 us  [ring_gather(): lax.ppermute(pieces[far - 1], axis, [(d, (d - 1) % ways) for d in range(w...]
    all_gather x1, blocking collectives: 13.7 us -> 18.9 us  [local(): lax.all_gather(kept_flag, 'ctx', axis=0, tiled=True)]
    dynamic_slice x12, local copies, waits for them, and re-layouts: 14 us -> 9.61 us  [advance(): lax.dynamic_slice_in_dim(member, offset, block_rows, 0)]
    while x32 -> x48, local copies, waits for them, and re-layouts: 0.07 us -> 4.28 us
    unnamed x18 -> x29, local copies, waits for them, and re-layouts: 4.96 us -> 4.57 us
  transfers between devices with their start and end apart: 3 -> 6, of which waited for: 2 -> 2; matrix products, arithmetic and copies ran while one was open for 16% -> 46% of each run, Pallas kernels for 0% -> 0%
where the time goes in v1:
time: 216 us
  matrix products  62.5 us (29%)
  blocking collectives  45.1 us (21%)
  waiting for transfers between devices  37.7 us (17%)
  other arithmetic  23.4 us (11%)
  local copies, waits for them, and re-layouts  21.8 us (10%)
  between operations  14.8 us (7%)
  starting transfers between devices  9.56 us (4%)
    ppermute x3, waiting for transfers between devices, ring_gather(): lax.ppermute(pieces[far - 1], axis, [(d, (d - 1) % ways) for d in range(w...  37.6 us
    all_gather x1, blocking collectives, local(): lax.all_gather(kept_flag, 'ctx', axis=0, tiled=True)  18.9 us
    dot_general x8, matrix products, block_scores(): jnp.einsum('gqd,tgd->gqt', query_rows, split_heads(key_block), preferred_...  16.3 us
    dot_general x8, matrix products, online_update(): jnp.einsum('gqt,tgd->gqd', weights.astype(jnp.bfloat16), value_heads, pre...  15.3 us
    reduce_sum x4, other arithmetic, online_update(): row_total = row_total * shrink + jnp.sum(weights, axis=2)  14.8 us
    dot_general x1, matrix products, local(): jnp.dot(grad_masked, out_weight.T, preferred_element_type=jnp.float32)  12.7 us
    unnamed x1, blocking collectives  11.5 us
    dynamic_slice x12, local copies, waits for them, and re-layouts, advance(): lax.dynamic_slice_in_dim(member, offset, block_rows, 0)  9.61 us
  transfers between devices with their start and end apart: 6, of which 2 were waited for; matrix products, arithmetic and copies ran while one was open for 46% of the time, Pallas kernels for 0%

profile of v1, /device:TPU:0, one launch (start us, length us, event | category | flops | bytes accessed | tf_op | source)
XLA Modules:
  0.0 215.6 jit_solution(11295653107064876547)
XLA Ops:
  7.2 2.0 copy.70
  9.3 1.3 copy.67
  10.6 5.1 %collective-permute-start = (bf16[512,512]{0,1:T(8,128)(2,1)S(1)}, bf16[512,512]{0,1:T(8,128)(2,1)S(1)}, u32[]{:S(2)}, u32[]{:S(2)}) collective-permute-start(bf16[512,512]{0,1:T(8,128)(2,1)S(1)} %copy.67), channel_id=1, source_target_pairs={{0,12},{4,0},{8,4},{12,8},{1,13},{5,1},{9,5},{13,9},{2,14},{6,2},{... | collective-permute-start | bytes 1572872 | tf_op jit(solution)/shard_map/ppermute | solution.py:17
  15.8 0.7 broadcast_compare_fusion.2
  16.4 17.8 %collective-permute-done = bf16[512,512]{0,1:T(8,128)(2,1)S(1)} collective-permute-done((bf16[512,512]{0,1:T(8,128)(2,1)S(1)}, bf16[512,512]{0,1:T(8,128)(2,1)S(1)}, u32[]{:S(2)}, u32[]{:S(2)}) %collective-permute-start) | collective-permute-done | bytes 524320 | tf_op jit(solution)/shard_map/ppermute | solution.py:17
  34.3 4.3 %collective-permute-start.1 = (bf16[512,512]{0,1:T(8,128)(2,1)S(1)}, bf16[512,512]{0,1:T(8,128)(2,1)S(1)}, u32[]{:S(2)}, u32[]{:S(2)}) collective-permute-start(bf16[512,512]{0,1:T(8,128)(2,1)S(1)} %collective-permute-done), channel_id=1, source_target_pairs={{0,12},{4,0},{8,4},{12,8},{1,13},{5,1},{9,5},{13,9},{2,14},{6,2},{... | collective-permute-start | bytes 1572872 | tf_op jit(solution)/shard_map/ppermute | solution.py:17
  38.6 12.7 %convolution_convert_fusion = bf16[128,2048]{1,0:T(8,128)(2,1)} fusion(bf16[2048,4096]{1,0:T(8,128)(2,1)} %param.15, bf16[128,4096]{1,0:T(8,128)(2,1)} %param.16, pred[128]{0:T(512)(128)(4,1)S(1)} %broadcast_compare_fusion.2), kind=kOutput, calls=%fused_computation.53 | convolution fusion | flops 2148270080 | bytes 18350208 | tf_op jit(solution)/shard_map/dot_general | solution.py:117
  51.4 19.7 %collective-permute-done.1 = bf16[512,512]{0,1:T(8,128)(2,1)S(1)} collective-permute-done((bf16[512,512]{0,1:T(8,128)(2,1)S(1)}, bf16[512,512]{0,1:T(8,128)(2,1)S(1)}, u32[]{:S(2)}, u32[]{:S(2)}) %collective-permute-start.1) | collective-permute-done | bytes 524320 | tf_op jit(solution)/shard_map/ppermute | solution.py:17
  71.2 0.4 reshape.201
  71.7 18.9 %all-gather = bf16[4,1,512]{2,1,0:T(2,128)(2,1)S(1)} all-gather(bf16[1,1,512]{2,1,0:T(2,128)(2,1)S(1)} %reshape.205), channel_id=1, replica_groups=mesh['groups'=2,'ctx'=4,'head'=2,'rep'=2] {'ctx'}, dimensions={0}, use_global_device_ids=true | all-gather | bytes 5120 | tf_op jit(solution)/shard_map/all_gather | solution.py:145
  90.7 1.4 reshape.203
  92.1 1.0 copy.73
  93.1 0.7 dynamic-slice
  95.2 54.8 %while.39 = (s32[]{:T(128)}, f32[4,512]{1,0:T(4,128)S(1)}, f32[4,512]{1,0:T(4,128)S(1)}, f32[4,512,128]{2,1,0:T(8,128)}, f32[4,512]{1,0:T(4,128)S(1)}, /*index=5...) while((s32[]{:T(128)}, f32[4,512]{1,0:T(4,128)S(1)}, ...), condition=%wide.region_6.7_spmd.clone, body=%wide.region_1.6_spmd.clone.sunk | while | flops 832591872 | bytes 61090668 | solution.py:92
  95.5 0.3 broadcast_compare_fusion.6
  95.9 3.4 %fusion.81 = (f32[4,512]{1,0:T(4,128)S(1)}, f32[4,512]{1,0:T(4,128)S(1)}, f32[4,512,512]{2,1,0:T(8,128)}) fusion(pred[512,512]{0,1:T(8,128)(4,1)S(1)} %get-tuple-element.631, pred[512,512]{0,1:T(8,128)(4,1)S(1)} %get-tuple-element.632, bf16[512,4,128]{0,2,1:T(8,128)(2,1)S(1)} %bitcast.121, bf16[4,512,128]{2,1,0:T(8,128)(2,1)S(1)} %get-tuple-element.682), kind=kOutput, calls=%fused_computation.19.clone.1 | convolution fusion | flops 273674240 | bytes 5783552 | tf_op jit(solution)/shard_map/while/body/eval_jaxpr/gqd,tgd->gqt/dot_general | solution.py:28
  99.3 3.7 %fusion.82 = (f32[4,512]{1,0:T(4,128)S(1)}, f32[4,512]{1,0:T(4,128)S(1)}) fusion(f32[4,512,512]{2,1,0:T(8,128)} %get-tuple-element.634, f32[4,512]{1,0:T(4,128)S(1)} %select_maximum_fusion.5, pred[512,512]{0,1:T(8,128)(4,1)S(1)} %get-tuple-element.631, f32[4,512]{1,0:T(4,128)S(1)} %select_maximum_fusion.4, pred[512,512]{0,1:T(8,128)(4,1)S(1)} %get-tuple-element.632), kind=kLoop, calls=%fused_computation.23.clone.1 | loop fusion | flops 9433088 | bytes 4751360 | tf_op jit(solution)/shard_map/while/body/eval_jaxpr/reduce_sum | solution.py:45
  103.1 1.1 constant_dynamic-slice_fusion.10
  104.2 1.9 fusion.85
  106.1 1.9 fusion.84
  108.1 1.0 copy-done.5
  109.2 0.3 broadcast_compare_fusion.6
  109.6 3.4 %fusion.81 = (f32[4,512]{1,0:T(4,128)S(1)}, f32[4,512]{1,0:T(4,128)S(1)}, f32[4,512,512]{2,1,0:T(8,128)}) fusion(pred[512,512]{0,1:T(8,128)(4,1)S(1)} %get-tuple-element.631, pred[512,512]{0,1:T(8,128)(4,1)S(1)} %get-tuple-element.632, bf16[512,4,128]{0,2,1:T(8,128)(2,1)S(1)} %bitcast.121, bf16[4,512,128]{2,1,0:T(8,128)(2,1)S(1)} %get-tuple-element.682), kind=kOutput, calls=%fused_computation.19.clone.1 | convolution fusion | flops 273674240 | bytes 5783552 | tf_op jit(solution)/shard_map/while/body/eval_jaxpr/gqd,tgd->gqt/dot_general | solution.py:28
  113.0 3.7 %fusion.82 = (f32[4,512]{1,0:T(4,128)S(1)}, f32[4,512]{1,0:T(4,128)S(1)}) fusion(f32[4,512,512]{2,1,0:T(8,128)} %get-tuple-element.634, f32[4,512]{1,0:T(4,128)S(1)} %select_maximum_fusion.5, pred[512,512]{0,1:T(8,128)(4,1)S(1)} %get-tuple-element.631, f32[4,512]{1,0:T(4,128)S(1)} %select_maximum_fusion.4, pred[512,512]{0,1:T(8,128)(4,1)S(1)} %get-tuple-element.632), kind=kLoop, calls=%fused_computation.23.clone.1 | loop fusion | flops 9433088 | bytes 4751360 | tf_op jit(solution)/shard_map/while/body/eval_jaxpr/reduce_sum | solution.py:45
  116.7 1.1 constant_dynamic-slice_fusion.10
  117.8 1.9 fusion.85
  119.8 1.9 fusion.84
  121.7 1.0 copy-done.5
  122.9 0.3 broadcast_compare_fusion.6
  123.2 3.4 %fusion.81 = (f32[4,512]{1,0:T(4,128)S(1)}, f32[4,512]{1,0:T(4,128)S(1)}, f32[4,512,512]{2,1,0:T(8,128)}) fusion(pred[512,512]{0,1:T(8,128)(4,1)S(1)} %get-tuple-element.631, pred[512,512]{0,1:T(8,128)(4,1)S(1)} %get-tuple-element.632, bf16[512,4,128]{0,2,1:T(8,128)(2,1)S(1)} %bitcast.121, bf16[4,512,128]{2,1,0:T(8,128)(2,1)S(1)} %get-tuple-element.682), kind=kOutput, calls=%fused_computation.19.clone.1 | convolution fusion | flops 273674240 | bytes 5783552 | tf_op jit(solution)/shard_map/while/body/eval_jaxpr/gqd,tgd->gqt/dot_general | solution.py:28
  126.6 3.7 %fusion.82 = (f32[4,512]{1,0:T(4,128)S(1)}, f32[4,512]{1,0:T(4,128)S(1)}) fusion(f32[4,512,512]{2,1,0:T(8,128)} %get-tuple-element.634, f32[4,512]{1,0:T(4,128)S(1)} %select_maximum_fusion.5, pred[512,512]{0,1:T(8,128)(4,1)S(1)} %get-tuple-element.631, f32[4,512]{1,0:T(4,128)S(1)} %select_maximum_fusion.4, pred[512,512]{0,1:T(8,128)(4,1)S(1)} %get-tuple-element.632), kind=kLoop, calls=%fused_computation.23.clone.1 | loop fusion | flops 9433088 | bytes 4751360 | tf_op jit(solution)/shard_map/while/body/eval_jaxpr/reduce_sum | solution.py:45
  130.4 1.1 constant_dynamic-slice_fusion.10
  131.5 1.9 fusion.85
  133.4 1.9 fusion.84
  135.4 1.0 copy-done.5
  136.5 0.3 broadcast_compare_fusion.6
  136.9 3.4 %fusion.81 = (f32[4,512]{1,0:T(4,128)S(1)}, f32[4,512]{1,0:T(4,128)S(1)}, f32[4,512,512]{2,1,0:T(8,128)}) fusion(pred[512,512]{0,1:T(8,128)(4,1)S(1)} %get-tuple-element.631, pred[512,512]{0,1:T(8,128)(4,1)S(1)} %get-tuple-element.632, bf16[512,4,128]{0,2,1:T(8,128)(2,1)S(1)} %bitcast.121, bf16[4,512,128]{2,1,0:T(8,128)(2,1)S(1)} %get-tuple-element.682), kind=kOutput, calls=%fused_computation.19.clone.1 | convolution fusion | flops 273674240 | bytes 5783552 | tf_op jit(solution)/shard_map/while/body/eval_jaxpr/gqd,tgd->gqt/dot_general | solution.py:28
  140.3 3.7 %fusion.82 = (f32[4,512]{1,0:T(4,128)S(1)}, f32[4,512]{1,0:T(4,128)S(1)}) fusion(f32[4,512,512]{2,1,0:T(8,128)} %get-tuple-element.634, f32[4,512]{1,0:T(4,128)S(1)} %select_maximum_fusion.5, pred[512,512]{0,1:T(8,128)(4,1)S(1)} %get-tuple-element.631, f32[4,512]{1,0:T(4,128)S(1)} %select_maximum_fusion.4, pred[512,512]{0,1:T(8,128)(4,1)S(1)} %get-tuple-element.632), kind=kLoop, calls=%fused_computation.23.clone.1 | loop fusion | flops 9433088 | bytes 4751360 | tf_op jit(solution)/shard_map/while/body/eval_jaxpr/reduce_sum | solution.py:45
  144.0 1.1 constant_dynamic-slice_fusion.10
  145.1 1.9 fusion.85
  147.1 1.9 fusion.84
  149.0 1.0 copy-done.5
  150.1 2.4 %multiply_reduce_fusion = (f32[4,512]{1,0:T(4,128)S(1)}, bf16[4,512,128]{2,1,0:T(8,128)(2,1)S(1)}) fusion(f32[4,512,128]{2,1,0:T(8,128)} %get-tuple-element.362, f32[4,512]{1,0:T(4,128)S(1)} %get-tuple-element.363, bf16[4,4,128,128]{3,2,1,0:T(8,128)(2,1)} %copy.73, f32[4,512,128]{2,1,0:T(8,128)} %get-tuple-element.360, f32[4,512]{1,0:T(4,128)S(1)} %get-tuple-element.361), kind=kLoop, calls=%fused_computation.55 | loop fusion | flops 1832960 | bytes 3170304 | tf_op jit(solution)/shard_map/reduce_sum | solution.py:151
  152.4 0.3 copy.71
  152.7 9.5 %fusion.39 = f32[128,4096]{1,0:T(8,128)} fusion(bf16[128,2048]{0,1:T(8,128)(2,1)S(1)} %bitcast.122, bf16[2048,4096]{1,0:T(8,128)(2,1)} %param.15), kind=kOutput, calls=%fused_computation.79 | convolution fusion | flops 2147483648 | bytes 19398656 | tf_op jit(solution)/shard_map/dot_general | solution.py:178
  162.4 18.1 %while.38 = (s32[]{:T(128)}, f32[2048]{0:T(1024)S(1)}, bf16[2048,512]{0,1:T(8,128)(2,1)}, bf16[4,512,128]{2,1,0:T(8,128)(2,1)S(1)}, f32[4,512]{1,0:T(4,128)S(1)}...) while((s32[]{:T(128)}, f32[2048]{0:T(1024)S(1)}, ...), condition=%wide.region_11.12_spmd.clone, body=%wide.region_9.11_spmd.clone.sunk | while | flops 546570752 | bytes 13140663 | solution.py:92
  162.4 1.3 constant_dynamic-slice_fusion.8
  163.7 0.7 fusion.73
  164.4 0.2 broadcast_compare_fusion.5
  164.6 2.1 fusion.74
  166.9 1.3 constant_dynamic-slice_fusion.8
  168.2 0.7 fusion.73
  169.1 2.1 fusion.74
  171.4 1.3 constant_dynamic-slice_fusion.8
  172.7 0.7 fusion.73
  173.6 2.1 fusion.74
  175.9 1.3 constant_dynamic-slice_fusion.8
  177.2 0.7 fusion.73
  178.2 2.1 fusion.74
  180.5 11.5 %all-reduce = f32[2048]{0:T(1024)S(1)} all-reduce(f32[2048]{0:T(1024)S(1)} %get-tuple-element.365), channel_id=3, replica_groups=mesh['groups'=2,'ctx'=4,'head'=2,'rep'=2] {'ctx'}, use_global_device_ids=true, to_apply=%region_12.13.clone | all-reduce | flops 2048 | bytes 16384
  192.0 5.6 %psum.14 = f32[512]{0:T(512)S(1)} all-reduce(f32[512]{0:T(512)S(1)} %dynamic-slice.1), channel_id=1, replica_groups=mesh['groups'=2,'ctx'=4,'head'=2,'rep'=2] {'head','rep'}, use_global_device_ids=true, to_apply=%region_13.14 | all-reduce | flops 512 | bytes 4096 | tf_op jit(solution)/shard_map/psum | solution.py:182
  197.7 0.3 convolution_bitcast_fusion
  198.0 9.1 %psum.15 = f32[32]{0:T(128)} all-reduce(f32[32]{0:T(128)S(1)} %convolution_bitcast_fusion), channel_id=1, replica_groups=mesh['groups'=2,'ctx'=4,'head'=2,'rep'=2] {'ctx'}, use_global_device_ids=true, to_apply=%region_14.15 | all-reduce | flops 32 | bytes 256 | tf_op jit(solution)/shard_map/psum | solution.py:186
  207.0 2.1 convert_element_type.44
  (139 shorter events, 3.5 us)
Async XLA Ops:
  7.2 88.1 %all-gather.4.cloned.1.call-start = ((), (), s32[]{:S(2)}) async-start(), calls=%async_computation.1 | async-start | bytes 2621440 | tf_op jit(solution)/shard_map/all_gather | solution.py:144
  9.3 153.1 %all-gather.6.cloned.1.call-start = ((), (), s32[]{:S(2)}) async-start(), calls=%async_computation.3 | async-start | bytes 2621440 | tf_op jit(solution)/shard_map/all_gather | solution.py:165
  10.6 5.1 %copy-start.1 = (bf16[512,512]{0,1:T(8,128)(2,1)}, bf16[512,512]{0,1:T(8,128)(2,1)S(1)}, u32[]{:S(2)}) copy-start(bf16[512,512]{0,1:T(8,128)(2,1)S(1)} %copy.67) | copy-start | bytes 1572868
  10.6 23.7 %collective-permute-start = (bf16[512,512]{0,1:T(8,128)(2,1)S(1)}, bf16[512,512]{0,1:T(8,128)(2,1)S(1)}, u32[]{:S(2)}, u32[]{:S(2)}) collective-permute-start(bf16[512,512]{0,1:T(8,128)(2,1)S(1)} %copy.67), channel_id=1, source_target_pairs={{0,12},{4,0},{8,4},{12,8},{1,13},{5,1},{9,5},{13,9},{2,14},{6,2},{... | collective-permute-start | bytes 1572872 | tf_op jit(solution)/shard_map/ppermute | solution.py:17
  15.7 191.3 %reduce-scatter.2.cloned.1.call-start = ((), (), s32[]{:S(2)}) async-start(), calls=%async_computation.2 | async-start | bytes 3145728 | tf_op jit(solution)/shard_map/reduce_scatter | solution.py:179
  16.4 34.8 %copy-start.9 = (s32[512]{0:T(512)S(1)}, s32[512]{0:T(512)}, u32[]{:S(2)}) copy-start(s32[512]{0:T(512)} %param.18) | copy-start | bytes 6148
  16.4 34.8 %copy-start.11 = (s32[4]{0:T(128)S(1)}, s32[4]{0:T(128)}, u32[]{:S(2)}) copy-start(s32[4]{0:T(128)} %param.19) | copy-start | bytes 52
  34.3 36.9 %copy-start.8 = (bf16[128,2048]{1,0:T(8,128)(2,1)S(1)}, bf16[128,2048]{1,0:T(8,128)(2,1)}, u32[]{:S(2)}) copy-start(bf16[128,2048]{1,0:T(8,128)(2,1)} %param.12) | copy-start | bytes 1572868
  34.3 36.8 %collective-permute-start.1 = (bf16[512,512]{0,1:T(8,128)(2,1)S(1)}, bf16[512,512]{0,1:T(8,128)(2,1)S(1)}, u32[]{:S(2)}, u32[]{:S(2)}) collective-permute-start(bf16[512,512]{0,1:T(8,128)(2,1)S(1)} %collective-permute-done), channel_id=1, source_target_pairs={{0,12},{4,0},{8,4},{12,8},{1,13},{5,1},{9,5},{13,9},{2,14},{6,2},{... | collective-permute-start | bytes 1572872 | tf_op jit(solution)/shard_map/ppermute | solution.py:17
  51.3 41.8 %copy-start.12 = (u32[32]{0:T(128)S(1)}, u32[32]{0:T(128)}, u32[]{:S(2)}) copy-start(u32[32]{0:T(128)} %constant.154) | copy-start | bytes 388
  51.3 43.1 %copy-start.2 = (bf16[512,512]{0,1:T(8,128)(2,1)S(1)}, bf16[512,512]{0,1:T(8,128)(2,1)}, u32[]{:S(2)}) copy-start(bf16[512,512]{0,1:T(8,128)(2,1)} %copy-done.1) | copy-start | bytes 1572868
  71.1 23.6 %collective-permute-start.2 = (bf16[512,512]{0,1:T(8,128)(2,1)S(1)}, bf16[512,512]{0,1:T(8,128)(2,1)S(1)}, u32[]{:S(2)}, u32[]{:S(2)}) collective-permute-start(bf16[512,512]{0,1:T(8,128)(2,1)S(1)} %collective-permute-done.1), channel_id=1, source_target_pairs={{0,12},{4,0},{8,4},{12,8},{1,13},{5,1},{9,5},{13,9},{2,14},{6,2},{... | collective-permute-start | bytes 1572872 | tf_op jit(solution)/shard_map/ppermute | solution.py:17
  99.3 4.9 %copy-start = (f32[4,512,512]{2,1,0:T(8,128)S(1)}, f32[4,512,512]{2,1,0:T(8,128)}, u32[]{:S(2)}) copy-start(f32[4,512,512]{2,1,0:T(8,128)} %get-tuple-element.634) | copy-start | bytes 12582916 | tf_op jit(solution)/shard_map/while
  99.3 4.9 %copy-start.6 = (f32[4,512,128]{2,1,0:T(8,128)S(1)}, f32[4,512,128]{2,1,0:T(8,128)}, u32[]{:S(2)}) copy-start(f32[4,512,128]{2,1,0:T(8,128)} %get-tuple-element.664) | copy-start | bytes 3145732 | tf_op jit(solution)/shard_map/while
  104.2 1.9 copy-start.4
  106.1 1.9 copy-start.7
  108.0 1.1 copy-start.5
  112.9 4.9 %copy-start = (f32[4,512,512]{2,1,0:T(8,128)S(1)}, f32[4,512,512]{2,1,0:T(8,128)}, u32[]{:S(2)}) copy-start(f32[4,512,512]{2,1,0:T(8,128)} %get-tuple-element.634) | copy-start | bytes 12582916 | tf_op jit(solution)/shard_map/while
  113.0 4.9 %copy-start.6 = (f32[4,512,128]{2,1,0:T(8,128)S(1)}, f32[4,512,128]{2,1,0:T(8,128)}, u32[]{:S(2)}) copy-start(f32[4,512,128]{2,1,0:T(8,128)} %get-tuple-element.664) | copy-start | bytes 3145732 | tf_op jit(solution)/shard_map/while
  117.8 1.9 copy-start.4
  119.8 1.9 copy-start.7
  121.7 1.1 copy-start.5
  126.6 4.9 %copy-start = (f32[4,512,512]{2,1,0:T(8,128)S(1)}, f32[4,512,512]{2,1,0:T(8,128)}, u32[]{:S(2)}) copy-start(f32[4,512,512]{2,1,0:T(8,128)} %get-tuple-element.634) | copy-start | bytes 12582916 | tf_op jit(solution)/shard_map/while
  126.6 4.9 %copy-start.6 = (f32[4,512,128]{2,1,0:T(8,128)S(1)}, f32[4,512,128]{2,1,0:T(8,128)}, u32[]{:S(2)}) copy-start(f32[4,512,128]{2,1,0:T(8,128)} %get-tuple-element.664) | copy-start | bytes 3145732 | tf_op jit(solution)/shard_map/while
  131.5 1.9 copy-start.4
  133.4 1.9 copy-start.7
  135.4 1.1 copy-start.5
  140.3 4.9 %copy-start = (f32[4,512,512]{2,1,0:T(8,128)S(1)}, f32[4,512,512]{2,1,0:T(8,128)}, u32[]{:S(2)}) copy-start(f32[4,512,512]{2,1,0:T(8,128)} %get-tuple-element.634) | copy-start | bytes 12582916 | tf_op jit(solution)/shard_map/while
  140.3 4.9 %copy-start.6 = (f32[4,512,128]{2,1,0:T(8,128)S(1)}, f32[4,512,128]{2,1,0:T(8,128)}, u32[]{:S(2)}) copy-start(f32[4,512,128]{2,1,0:T(8,128)} %get-tuple-element.664) | copy-start | bytes 3145732 | tf_op jit(solution)/shard_map/while
  145.1 1.9 copy-start.4
  147.1 1.9 copy-start.7
  149.0 1.1 copy-start.5
  152.7 9.6 %copy-start.3 = (bf16[4,4,128,128]{3,2,1,0:T(8,128)(2,1)S(1)}, bf16[4,4,128,128]{3,2,1,0:T(8,128)(2,1)}, u32[]{:S(2)}) copy-start(bf16[4,4,128,128]{3,2,1,0:T(8,128)(2,1)} %copy.73) | copy-start | bytes 1572868
  197.7 11.4 %copy-start.10 = (f32[512]{0:T(512)}, f32[512]{0:T(512)S(1)}, u32[]{:S(2)}) copy-start(f32[512]{0:T(512)S(1)} %psum.14) | copy-start | bytes 6148
Sparse Core Ops, SparseCore 0:
  9.6 65.5 all-gather.3
  77.3 48.8 all-gather.5
  162.4 32.3 reduce-scatter.1
